TPU v7x, 32 devices: a whole 2x2x4 slice. The times are simulated.
32 devices in a mesh: expert: 8 (over z, y), shard: 4 (over x, core).
Axes of the slice: x: 2, y: 2, z: 4, core: 2. Of those that a mesh axis runs over, the one named last changes fastest.
Arguments:
- tokens: float32 [25216, 512], P(('expert', 'shard')), may hold values from -6 to 6
- routes: int32 [25216, 2], P(('expert', 'shard')), may hold values from 0 to 7, all different within a row; in each aligned block of 394 rows (0 to 393, 394 to 787, ...) at most 192 rows name the same one
- priority: int32 [25216], P(('expert', 'shard')), may hold values from 0 to 393, as said below
- norm_gain: bfloat16 [2, 2, 512], P(None, None, 'shard'), may hold values from 0.5 to 1.5
- norm_bias: bfloat16 [2, 2, 512], P(None, None, 'shard'), may hold values from -1 to 1
- w_qkv: bfloat16 [2, 512, 1536], P(None, 'shard'), may hold values from -0.25 to 0.25
- w_proj: bfloat16 [2, 512, 512], P(None, 'shard'), may hold values from -2 to 2
- w_router: bfloat16 [2, 512, 8], P(None, 'shard'), may hold values from -0.1875 to 0.1875
- exp_in: bfloat16 [2, 8, 512, 2048], P(None, 'expert', 'shard'), may hold values from -0.25 to 0.25
- exp_out: bfloat16 [2, 8, 2048, 512], P(None, 'expert', 'shard'), may hold values from -0.875 to 0.875
- cotangent: float32 [25216, 512], P(('expert', 'shard')), may hold values from -6 to 6
Outputs:
- activations: float32 [25216, 512], P(('expert', 'shard'))
- d_tokens: float32 [25216, 512], P(('expert', 'shard'))
- grad_gain: float32 [2, 2, 512], P(None, None, 'shard')
- grad_bias: float32 [2, 2, 512], P(None, None, 'shard')
- grad_qkv: float32 [2, 512, 1536], P(None, 'shard')
- grad_proj: float32 [2, 512, 512], P(None, 'shard')
- grad_router: float32 [2, 512, 8], P(None, 'shard')
- grad_exp_in: float32 [2, 8, 512, 2048], P(None, 'expert', 'shard')
- grad_exp_out: float32 [2, 8, 2048, 512], P(None, 'expert', 'shard')
Inputs may be any that keep to these rules, and one draw needn't show every extreme that they name: `routes`: each row names 2 different experts; in each aligned block of 394 rows no expert is named by more than 192 rows. `priority`: in each aligned block of 394 rows the values are a permutation of 0 to 393.
All inputs are finite; a program needn't handle non-finite values.
Results may differ from a plain program's by a relative error of at most 0.025.
Values may be sent and summed in bfloat16 or wider, within the bound.
No kernel may reach another device: no remote copies, remote signals or barrier semaphores. Data moves between devices by JAX's collectives and lax.ppermute only.
A program may use at most 256 MiB of HBM per device.

v0:
```python
import jax
import jax.numpy as jnp
from jax import lax
from jax.sharding import PartitionSpec as P

D = 512
HEADS = 8
HEAD = 64
HIDDEN_SIZE = 2048
EXP_DEV = 1
SEQ = 197
MICRO = 2
LAYERS = 2
TOP = 2
TOK_MB = 394
norm_eps = 1e-06


def layer_norm(values, norm_scale, norm_shift):
    centre = values - jnp.mean(values, axis=-1, keepdims=True)
    spread = jnp.mean(centre * centre, axis=-1, keepdims=True)
    return centre * lax.rsqrt(spread + norm_eps) * norm_scale + norm_shift


def gelu_tanh(values):
    return jax.nn.gelu(values, approximate=True)


def dot_first(left, right):
    return lax.dot_general(
        left, right, (((0,), (0,)), ((), ())), preferred_element_type=jnp.float32
    )


def dot_last(left, right):
    return lax.dot_general(
        left, right, (((1,), (1,)), ((), ())), preferred_element_type=jnp.float32
    )


def slot_tables(route_ids, prio_rank, experts, capacity):
    tok_count = route_ids.shape[0]
    order_key = jnp.concatenate([prio_rank, prio_rank + tok_count])
    pair_expert = jnp.concatenate([route_ids[:, 0], route_ids[:, 1]])
    same_expert = pair_expert[:, None] == pair_expert[None, :]
    earlier = order_key[None, :] < order_key[:, None]
    position = jnp.sum((same_expert & earlier).astype(jnp.int32), axis=1)
    kept_mask = position < capacity
    flat_slot = jnp.where(kept_mask, pair_expert * capacity + position, experts * capacity)
    pair_ids = jnp.arange(2 * tok_count, dtype=jnp.int32)
    slot_pair = (
        jnp.full((experts * capacity + 1,), 2 * tok_count, jnp.int32).at[flat_slot].set(pair_ids)
    )
    slot_pair = slot_pair[: experts * capacity]
    slot_token = jnp.where(slot_pair < 2 * tok_count, slot_pair % tok_count, tok_count)
    return (flat_slot, slot_pair, slot_token, kept_mask)


def block_tables(route_ids, prio_rank, experts, capacity):
    blocks, tok_count = prio_rank.shape
    flat_slot, slot_pair, slot_token, kept_mask = jax.vmap(
        lambda r, p: slot_tables(r, p, experts, capacity)
    )(route_ids, prio_rank)
    block_ids = jnp.arange(blocks, dtype=jnp.int32)
    send_index = (
        (block_ids[:, None] * (tok_count + 1) + slot_token)
        .reshape(blocks, experts, capacity)
        .transpose(1, 0, 2)
    )
    pair_index = (
        (block_ids[:, None] * (2 * tok_count + 1) + slot_pair)
        .reshape(blocks, experts, capacity)
        .transpose(1, 0, 2)
    )
    slot_e = flat_slot // capacity
    slot_c = flat_slot % capacity
    back_index = jnp.where(
        kept_mask,
        (slot_e * blocks + block_ids[:, None]) * capacity + slot_c,
        experts * blocks * capacity,
    )
    return (send_index, pair_index, back_index, kept_mask)


def forward_layer(residual, route_hot, tables, weights, experts, capacity):
    norm_gains, norm_shifts, qkv_w, proj_w, router_w, in_w, out_w = weights
    send_index, pair_index, back_index, kept_mask = tables
    tok_count = residual.shape[0]
    blocks = back_index.shape[0]
    tok_block = tok_count // blocks
    seq_count = tok_count // SEQ
    score_scale = HEAD ** (-0.5)
    norm_scale = norm_gains.astype(jnp.float32)
    norm_shift = norm_shifts.astype(jnp.float32)
    normed = layer_norm(residual, norm_scale[0], norm_shift[0]).astype(jnp.bfloat16)
    qkv_rows = jnp.dot(normed, qkv_w, preferred_element_type=jnp.float32).astype(jnp.bfloat16)
    heads = qkv_rows.reshape(seq_count, SEQ, 3, HEADS, HEAD)
    scores = (
        jnp.einsum(
            "sqhd,skhd->shqk", heads[:, :, 0], heads[:, :, 1], preferred_element_type=jnp.float32
        )
        * score_scale
    )
    row_top = jnp.max(scores, axis=-1, keepdims=True)
    scores_exp = jnp.exp(scores - row_top)
    row_total = jnp.sum(scores_exp, axis=-1, keepdims=True)
    soft_scores = scores_exp / row_total
    log_total = row_top + jnp.log(row_total)
    mixed_heads = jnp.einsum(
        "shqk,skhd->sqhd",
        soft_scores.astype(jnp.bfloat16),
        heads[:, :, 2],
        preferred_element_type=jnp.float32,
    )
    mixed_heads = mixed_heads.astype(jnp.bfloat16).reshape(tok_count, D)
    middle = residual + jnp.dot(mixed_heads, proj_w, preferred_element_type=jnp.float32)
    normed_two = layer_norm(middle, norm_scale[1], norm_shift[1]).astype(jnp.bfloat16)
    gate_probs = jax.nn.softmax(
        jnp.dot(normed_two, router_w, preferred_element_type=jnp.float32), axis=-1
    )
    padded = jnp.concatenate(
        [normed_two.reshape(blocks, tok_block, D), jnp.zeros((blocks, 1, D), jnp.bfloat16)], axis=1
    ).reshape(blocks * (tok_block + 1), D)
    sending = padded[send_index]
    received = lax.all_to_all(sending, "expert", split_axis=0, concat_axis=0, tiled=True)
    row_block = received.reshape(experts * blocks * capacity, D)
    hidden_pre = jnp.dot(row_block, in_w[0], preferred_element_type=jnp.float32)
    hidden_act = gelu_tanh(hidden_pre).astype(jnp.bfloat16)
    expert_rows = jnp.dot(hidden_act, out_w[0], preferred_element_type=jnp.float32).astype(
        jnp.bfloat16
    )
    returned = lax.all_to_all(
        expert_rows.reshape(experts, blocks, capacity, D),
        "expert",
        split_axis=0,
        concat_axis=0,
        tiled=True,
    )
    back_rows = jnp.concatenate(
        [returned.reshape(experts * blocks * capacity, D), jnp.zeros((1, D), jnp.bfloat16)]
    )
    pair_rows = back_rows[back_index].astype(jnp.float32).reshape(blocks, TOP, tok_block, D)
    probs_block = gate_probs.reshape(blocks, tok_block, experts)
    chosen = jnp.sum(route_hot * probs_block[:, :, None, :], axis=-1)
    kept_gate = kept_mask.astype(jnp.float32).reshape(blocks, TOP, tok_block)
    weight_pair = kept_gate * chosen.transpose(0, 2, 1)
    combined = jnp.sum(weight_pair[..., None] * pair_rows, axis=1)
    output = middle + combined.reshape(tok_count, D)
    saved_state = (
        residual,
        normed,
        heads,
        log_total,
        mixed_heads,
        middle,
        normed_two,
        gate_probs,
        kept_gate,
        weight_pair,
        pair_rows,
        row_block,
        hidden_pre,
    )
    return (output, saved_state)


def backward_layer(d_output, saved_state, route_hot, tables, weights, experts, capacity):
    (
        residual,
        normed,
        heads,
        log_total,
        mixed_heads,
        middle,
        normed_two,
        gate_probs,
        kept_gate,
        weight_pair,
        pair_rows,
        row_block,
        hidden_pre,
    ) = saved_state
    send_index, pair_index, back_index, kept_mask = tables
    norm_gains, norm_shifts, qkv_w, proj_w, router_w, in_w, out_w = weights
    tok_count = residual.shape[0]
    blocks = back_index.shape[0]
    tok_block = tok_count // blocks
    seq_count = tok_count // SEQ
    score_scale = HEAD ** (-0.5)
    norm_scale = norm_gains.astype(jnp.float32)
    norm_shift = norm_shifts.astype(jnp.float32)
    d_block = d_output.reshape(blocks, 1, tok_block, D)
    d_gate_pair = kept_gate * jnp.sum(d_block * pair_rows, axis=-1)
    d_gates = jnp.sum(route_hot * d_gate_pair.transpose(0, 2, 1)[..., None], axis=2)
    d_gates = d_gates.reshape(tok_count, experts)
    d_logits = (
        gate_probs * (d_gates - jnp.sum(gate_probs * d_gates, axis=-1, keepdims=True))
    ).astype(jnp.bfloat16)
    g_router = dot_first(normed_two, d_logits)
    d_normed_two = dot_last(d_logits, router_w)
    d_pairs = (
        (weight_pair[..., None] * d_block).astype(jnp.bfloat16).reshape(blocks, TOP * tok_block, D)
    )
    d_pairs = jnp.concatenate([d_pairs, jnp.zeros((blocks, 1, D), jnp.bfloat16)], axis=1).reshape(
        blocks * (TOP * tok_block + 1), D
    )
    d_slots = d_pairs[pair_index]
    d_expert_out = lax.all_to_all(d_slots, "expert", split_axis=0, concat_axis=0, tiled=True)
    flat_out = d_expert_out.reshape(experts * blocks * capacity, D)
    hidden_act = gelu_tanh(hidden_pre).astype(jnp.bfloat16)
    g_out = dot_first(hidden_act, flat_out)
    d_act = dot_last(flat_out, out_w[0])
    d_pre = jax.vjp(gelu_tanh, hidden_pre)[1](d_act)[0].astype(jnp.bfloat16)
    g_in = dot_first(row_block, d_pre)
    d_rows = dot_last(d_pre, in_w[0]).astype(jnp.bfloat16).reshape(experts, blocks, capacity, D)
    d_back = lax.all_to_all(d_rows, "expert", split_axis=0, concat_axis=0, tiled=True)
    d_pair_in = jnp.concatenate(
        [d_back.reshape(experts * blocks * capacity, D), jnp.zeros((1, D), jnp.bfloat16)]
    )[back_index]
    d_pair_in = d_pair_in.astype(jnp.float32).reshape(blocks, TOP, tok_block, D)
    d_normed_two = d_normed_two + jnp.sum(d_pair_in, axis=1).reshape(tok_count, D)
    pulled_two = jax.vjp(layer_norm, middle, norm_scale[1], norm_shift[1])[1](d_normed_two)
    d_middle = d_output + pulled_two[0]
    d_branch = d_middle.astype(jnp.bfloat16)
    g_proj = dot_first(mixed_heads, d_branch)
    d_mixed = dot_last(d_branch, proj_w).astype(jnp.bfloat16).reshape(seq_count, SEQ, HEADS, HEAD)
    query_heads = heads[:, :, 0]
    key_heads = heads[:, :, 1]
    value_heads = heads[:, :, 2]
    scores = (
        jnp.einsum("sqhd,skhd->shqk", query_heads, key_heads, preferred_element_type=jnp.float32)
        * score_scale
    )
    soft_scores = jnp.exp(scores - log_total)
    d_soft = jnp.einsum("sqhd,skhd->shqk", d_mixed, value_heads, preferred_element_type=jnp.float32)
    d_values = jnp.einsum(
        "shqk,sqhd->skhd",
        soft_scores.astype(jnp.bfloat16),
        d_mixed,
        preferred_element_type=jnp.float32,
    )
    d_scores = (
        soft_scores * (d_soft - jnp.sum(soft_scores * d_soft, axis=-1, keepdims=True))
    ).astype(jnp.bfloat16)
    d_query = (
        jnp.einsum("shqk,skhd->sqhd", d_scores, key_heads, preferred_element_type=jnp.float32)
        * score_scale
    )
    d_keys = (
        jnp.einsum("shqk,sqhd->skhd", d_scores, query_heads, preferred_element_type=jnp.float32)
        * score_scale
    )
    d_qkv = (
        jnp.stack([d_query, d_keys, d_values], axis=2)
        .reshape(tok_count, 3 * D)
        .astype(jnp.bfloat16)
    )
    g_qkv = dot_first(normed, d_qkv)
    d_normed = dot_last(d_qkv, qkv_w)
    pulled_one = jax.vjp(layer_norm, residual, norm_scale[0], norm_shift[0])[1](d_normed)
    d_residual = d_middle + pulled_one[0]
    g_gain = jnp.stack([pulled_one[1], pulled_two[1]])
    g_shift = jnp.stack([pulled_one[2], pulled_two[2]])
    return (d_residual, (g_gain, g_shift, g_qkv, g_proj, g_router, g_in[None], g_out[None]))


SCATTER_DIMS = (1, 1, 0, 0, 0, 1, 1)


def reduce_layer(layer_grads):
    scattered = [
        lax.psum_scatter(
            grad.astype(jnp.bfloat16), "shard", scatter_dimension=dim, tiled=True
        ).astype(jnp.float32)
        for grad, dim in zip(layer_grads, SCATTER_DIMS)
    ]
    replicated = [
        lax.psum(part.astype(jnp.bfloat16), "expert").astype(jnp.float32) for part in scattered[:5]
    ]
    return replicated + scattered[5:]


def local(
    tokens,
    routes,
    priority,
    norm_gain,
    norm_bias,
    w_qkv,
    w_proj,
    w_router,
    exp_in,
    exp_out,
    cotangent,
):
    experts = lax.axis_size("expert") * EXP_DEV
    capacity = max(8, (5 * TOK_MB // (2 * experts) + 7) // 8 * 8)
    tok_count = tokens.shape[0]
    blocks = tok_count // TOK_MB
    route_ids = routes.reshape(blocks, TOK_MB, TOP)
    prio_rank = priority.reshape(blocks, TOK_MB)
    tables = block_tables(route_ids, prio_rank, experts, capacity)
    route_hot = (route_ids[..., None] == jnp.arange(experts, dtype=jnp.int32)).astype(jnp.float32)
    all_weights = []
    for layer_index in range(LAYERS):
        all_weights.append(
            (
                lax.all_gather(norm_gain[layer_index], "shard", axis=1, tiled=True),
                lax.all_gather(norm_bias[layer_index], "shard", axis=1, tiled=True),
                lax.all_gather(w_qkv[layer_index], "shard", axis=0, tiled=True),
                lax.all_gather(w_proj[layer_index], "shard", axis=0, tiled=True),
                lax.all_gather(w_router[layer_index], "shard", axis=0, tiled=True),
                lax.all_gather(exp_in[layer_index], "shard", axis=1, tiled=True),
                lax.all_gather(exp_out[layer_index], "shard", axis=1, tiled=True),
            )
        )
    residual = tokens
    saved_list = []
    for layer_index in range(LAYERS):
        residual, saved_state = forward_layer(
            residual, route_hot, tables, all_weights[layer_index], experts, capacity
        )
        saved_list.append(saved_state)
    activations = residual
    d_residual = cotangent
    reduced = [None] * LAYERS
    for layer_index in reversed(range(LAYERS)):
        d_residual, layer_grads = backward_layer(
            d_residual,
            saved_list[layer_index],
            route_hot,
            tables,
            all_weights[layer_index],
            experts,
            capacity,
        )
        reduced[layer_index] = reduce_layer(layer_grads)
    outs = [jnp.stack([reduced[l][k] for l in range(LAYERS)]) for k in range(7)]
    return (activations, d_residual, *outs)


def solution(mesh):
    return jax.shard_map(
        local,
        mesh=mesh,
        in_specs=(
            P(("expert", "shard"), None),
            P(("expert", "shard"), None),
            P(("expert", "shard")),
            P(None, None, "shard"),
            P(None, None, "shard"),
            P(None, "shard", None),
            P(None, "shard", None),
            P(None, "shard", None),
            P(None, "expert", "shard", None),
            P(None, "expert", "shard", None),
            P(("expert", "shard"), None),
        ),
        out_specs=(
            P(("expert", "shard"), None),
            P(("expert", "shard"), None),
            P(None, None, "shard"),
            P(None, None, "shard"),
            P(None, "shard", None),
            P(None, "shard", None),
            P(None, "shard", None),
            P(None, "expert", "shard", None),
            P(None, "expert", "shard", None),
        ),
        check_vma=False,
    )
```

profile of v0, /device:TPU:0, one launch (start us, length us, event | category | flops | bytes accessed | tf_op | source)
XLA Modules:
  0.0 1172.4 jit_solution(14263850944963940253)
XLA Ops:
  24.2 16.5 %fusion.16 = s32[2,788]{0,1:T(8,128)S(1)} fusion(s32[2,788]{0,1:T(8,128)S(1)} %copy.267, s32[2,788]{1,0:T(2,128)S(1)} %get-tuple-element.105, s32[2,788]{1,0:T(2,128)S(1)} %get-tuple-element.104, s32[2,788]{0,1:T(8,128)S(1)} %copy.266), kind=kLoop, calls=%fused_computation.42 | loop fusion | flops 6207864 | bytes 31520 | tf_op jit(solution)/shard_map/vmap()/reduce_sum | solution.py:47
  44.0 8.8 scatter_custom_fusion
  53.0 8.3 all-gather.3
  65.7 7.2 reshape.713
  98.6 9.2 gather_fusion
  107.8 6.1 all-to-all-start
  115.2 47.6 %all-to-all-done = bf16[8,2,128,512]{3,2,1,0:T(8,128)(2,1)} async-done(((bf16[8,2,128,512]{3,2,1,0:T(8,128)(2,1)}), bf16[8,2,128,512]{3,2,1,0:T(8,128)(2,1)}, u32[]{:S(2)}, u32[]{:S(2)}) %all-to-all-start) | async-done | bytes 2097184 | tf_op jit(solution)/shard_map/all_to_all | solution.py:125
  162.8 14.2 %multiply_convert_fusion.1 = (bf16[2048,2048]{1,0:T(8,128)(2,1)}, f32[2048,2048]{1,0:T(8,128)}) fusion(bf16[2048,512]{1,0:T(8,128)(2,1)} %bitcast.20, bf16[1,1,512,2048]{3,2,1,0:T(8,128)(2,1)} %all-gather.23.cloned.1.call-done), kind=kOutput, calls=%fused_computation.28 | convolution fusion | flops 4332716032 | bytes 29360128 | tf_op jit(solution)/shard_map/dot_general | solution.py:127
  176.9 9.8 convolution_convert_fusion.11
  207.9 9.0 all-gather.10
  218.7 20.5 %all-to-all-done.1 = bf16[8,2,128,512]{3,2,1,0:T(8,128)(2,1)} async-done(((bf16[8,2,128,512]{3,2,1,0:T(8,128)(2,1)}), bf16[8,2,128,512]{3,2,1,0:T(8,128)(2,1)}, u32[]{:S(2)}, u32[]{:S(2)}) %all-to-all-start.1) | async-done | bytes 2097184 | tf_op jit(solution)/shard_map/all_to_all | solution.py:132
  240.9 6.4 gather_fusion.1
  261.7 7.2 reshape.714
  294.1 9.2 gather_fusion.2
  323.8 9.2 gather_fusion.4
  333.0 22.5 %all-to-all-done.2 = bf16[8,2,128,512]{3,2,1,0:T(8,128)(2,1)} async-done(((bf16[8,2,128,512]{3,2,1,0:T(8,128)(2,1)}), bf16[8,2,128,512]{3,2,1,0:T(8,128)(2,1)}, u32[]{:S(2)}, u32[]{:S(2)}) %all-to-all-start.2) | async-done | bytes 2097184 | tf_op jit(solution)/shard_map/all_to_all | solution.py:125
  359.7 14.4 %multiply_convert_fusion = (bf16[2048,2048]{1,0:T(8,128)(2,1)}, f32[2048,2048]{1,0:T(8,128)}) fusion(bf16[2048,512]{1,0:T(8,128)(2,1)} %bitcast.38, bf16[1,1,512,2048]{3,2,1,0:T(8,128)(2,1)} %all-gather.29.cloned.1.call-done), kind=kOutput, calls=%fused_computation.27 | convolution fusion | flops 4332716032 | bytes 29360128 | tf_op jit(solution)/shard_map/dot_general | solution.py:127
  374.1 11.0 all-gather.31.cloned.1.call-done
  385.1 22.4 %all-to-all-done.4 = bf16[8,2,128,512]{3,2,1,0:T(8,128)(2,1)S(1)} async-done(((bf16[8,2,128,512]{3,2,1,0:T(8,128)(2,1)}), bf16[8,2,128,512]{3,2,1,0:T(8,128)(2,1)S(1)}, u32[]{:S(2)}, u32[]{:S(2)}) %all-to-all-start.4) | async-done | bytes 2097184 | tf_op jit(solution)/shard_map/all_to_all | solution.py:208
  407.5 17.1 %fusion.13 = bf16[2048,2048]{1,0:T(8,128)(2,1)S(1)} fusion(f32[2048,2048]{1,0:T(8,128)} %get-tuple-element.95, bf16[2048,512]{1,0:T(8,128)(2,1)S(1)} %bitcast.301, bf16[1,1,2048,512]{3,2,1,0:T(8,128)(2,1)} %all-gather.31.cloned.1.call-done), kind=kOutput, calls=%fused_computation.26 | convolution fusion | flops 4378853376 | bytes 29360128 | tf_op jit(solution)/shard_map/dot_general | solution.py:36
  424.7 6.1 convolution_convert_fusion.9
  434.3 9.8 convolution_convert_fusion.10
  444.2 38.6 %all-to-all-done.5 = bf16[8,2,128,512]{3,2,1,0:T(8,128)(2,1)S(1)} async-done(((bf16[8,2,128,512]{3,2,1,0:T(8,128)(2,1)}), bf16[8,2,128,512]{3,2,1,0:T(8,128)(2,1)S(1)}, u32[]{:S(2)}, u32[]{:S(2)}) %all-to-all-start.5) | async-done | bytes 2097184 | tf_op jit(solution)/shard_map/all_to_all | solution.py:216
  490.5 6.0 gather_fusion.5
  496.5 39.9 %all-to-all-done.3 = bf16[8,2,128,512]{3,2,1,0:T(8,128)(2,1)} async-done(((bf16[8,2,128,512]{3,2,1,0:T(8,128)(2,1)}), bf16[8,2,128,512]{3,2,1,0:T(8,128)(2,1)}, u32[]{:S(2)}, u32[]{:S(2)}) %all-to-all-start.3) | async-done | bytes 2097184 | tf_op jit(solution)/shard_map/all_to_all | solution.py:132
  538.2 6.0 gather_fusion.3
  587.8 7.0 convert_element_type.280
  609.2 9.2 gather_fusion.6
  618.4 52.1 %all_to_all.40 = bf16[8,2,128,512]{3,2,1,0:T(8,128)(2,1)S(1)} all-to-all(bf16[8,2,128,512]{3,2,1,0:T(8,128)(2,1)} %bitcast.299), channel_id=1, replica_groups=mesh['expert'=8,'shard'=4] {'expert'}, dimensions={0} | all-to-all | bytes 4194304 | tf_op jit(solution)/shard_map/all_to_all | solution.py:208
  670.5 17.5 %fusion.6 = bf16[2048,2048]{1,0:T(8,128)(2,1)S(1)} fusion(f32[2048,2048]{1,0:T(8,128)} %get-tuple-element.85, bf16[2048,512]{1,0:T(8,128)(2,1)S(1)} %bitcast.303, bf16[1,1,2048,512]{3,2,1,0:T(8,128)(2,1)S(1)} %copy-done.103), kind=kOutput, calls=%fused_computation.19 | convolution fusion | flops 4378853376 | bytes 29360128 | tf_op jit(solution)/shard_map/dot_general | solution.py:36
  688.0 6.1 convolution_convert_fusion.8
  714.5 31.5 %all-to-all-done.7 = bf16[8,2,128,512]{3,2,1,0:T(8,128)(2,1)} async-done(((bf16[8,2,128,512]{3,2,1,0:T(8,128)(2,1)}), bf16[8,2,128,512]{3,2,1,0:T(8,128)(2,1)}, u32[]{:S(2)}, u32[]{:S(2)}) %all-to-all-start.7) | async-done | bytes 2097184 | tf_op jit(solution)/shard_map/all_to_all | solution.py:216
  781.3 6.4 multiply_convert_fusion.2
  795.3 6.9 convert_element_type.291
  814.6 9.9 fusion.32
  824.5 10.1 fusion.31
  834.8 9.9 fusion.30
  844.8 9.9 fusion.29
  861.5 7.6 reduce-scatter.31.cloned.1.call-done
  869.1 30.4 %reduce-scatter.27.cloned.1.call-done = bf16[128,1536]{1,0:T(8,128)(2,1)} async-done(((bf16[512,1536]{1,0:T(8,128)(2,1)}), bf16[128,1536]{1,0:T(8,128)(2,1)}) %reduce-scatter.27.cloned.1.call-update) | async-done | bytes 393232 | tf_op jit(solution)/shard_map/reduce_scatter | solution.py:272
  902.3 19.1 %reduce-scatter.47.cloned.1.call-done = bf16[128,2]{1,0:T(8,128)(2,1)} async-done(((bf16[512,2]{1,0:T(8,128)(2,1)}), bf16[128,2]{1,0:T(8,128)(2,1)}) %reduce-scatter.47.cloned.1.call-update) | async-done | bytes 528
  922.2 21.1 %reduce-scatter.43.cloned.1.call-done = bf16[128,2]{1,0:T(8,128)(2,1)} async-done(((bf16[512,2]{1,0:T(8,128)(2,1)}), bf16[128,2]{1,0:T(8,128)(2,1)}) %reduce-scatter.43.cloned.1.call-update) | async-done | bytes 528
  944.2 21.6 %all-reduce.8 = (bf16[1,2,128]{2,1,0:T(2,128)(2,1)S(1)}, bf16[1,2,128]{2,1,0:T(2,128)(2,1)S(1)}, bf16[1,2,128]{2,1,0:T(2,128)(2,1)S(1)}, bf16[1,2,128]{2,1,0:T(2...) all-reduce(bf16[1,2,128]{2,1,0:T(2,128)(2,1)S(1)} %bitcast.346, ...), channel_id=1, replica_groups=mesh['expert'=8,'shard'=4] {'expert'}, use_global_device_ids=true, to_apply=%region_47.48 | all-reduce | flops 3072 | bytes 12288 | tf_op jit(solution)/shard_map/psum | solution.py:278
  967.6 9.9 reduce-scatter.41.cloned.1.call-done
  977.5 33.6 %reduce-scatter.39.cloned.1.call-done = bf16[1,512,512]{2,1,0:T(8,128)(2,1)} async-done(((bf16[1,2048,512]{2,1,0:T(8,128)(2,1)}), bf16[1,512,512]{2,1,0:T(8,128)(2,1)}) %reduce-scatter.39.cloned.1.call-update) | async-done | bytes 524304 | tf_op jit(solution)/shard_map/reduce_scatter | solution.py:272
  1013.8 31.7 %reduce-scatter.37.cloned.1.call-done = bf16[1,128,2048]{2,1,0:T(8,128)(2,1)} async-done(((bf16[1,512,2048]{2,1,0:T(8,128)(2,1)}), bf16[1,128,2048]{2,1,0:T(8,128)(2,1)}) %reduce-scatter.37.cloned.1.call-update) | async-done | bytes 524304 | tf_op jit(solution)/shard_map/reduce_scatter | solution.py:272
  1045.4 33.6 %reduce-scatter.35.cloned.1.call-done = bf16[1,128,2048]{2,1,0:T(8,128)(2,1)} async-done(((bf16[1,512,2048]{2,1,0:T(8,128)(2,1)}), bf16[1,128,2048]{2,1,0:T(8,128)(2,1)}) %reduce-scatter.35.cloned.1.call-update) | async-done | bytes 524304 | tf_op jit(solution)/shard_map/reduce_scatter | solution.py:272
  1081.7 79.5 %all-reduce.12.cloned.1.call-done = (bf16[1,128,1536]{2,1,0:T(8,128)(2,1)}, bf16[1,128,1536]{2,1,0:T(8,128)(2,1)}, bf16[1,128,512]{2,1,0:T(8,128)(2,1)}, bf16[1,128,512]{2,1,0:T(8,128)(2,1)}) async-done(((bf16[1,128,1536]{2,1,0:T(8,128)(2,1)}, bf16[1,128,1536]{2,1,0:T(8,128)(2,1)}, bf16[1,128,512]{2,1,0:T(8,128)(2,1)}, bf16[1,128,512]{2,1,0:T(8,128)(2,1)}), (bf16[1,128,1536]{2,1,0:T(8,128)(2,1)}, ...) | async-done | bytes 1048592 | tf_op jit(solution)/shard_map/psum | solution.py:278
  (517 shorter events, 308.4 us)
Async XLA Ops:
  7.2 54.0 %all-gather.21.cloned.1.call-start = ((), (), s32[]{:S(2)}) async-start(), calls=%async_computation.30 | async-start | bytes 1966080 | tf_op jit(solution)/shard_map/all_gather | solution.py:310
  9.5 105.7 %all-gather.23.cloned.1.call-start = ((), (), s32[]{:S(2)}) async-start(), calls=%async_computation.31 | async-start | bytes 2621440 | tf_op jit(solution)/shard_map/all_gather | solution.py:313
  22.1 39.2 %copy-start.87 = (f32[1,1,512]{2,1,0:T(1,128)}, f32[1,1,512]{2,1,0:T(1,128)S(1)}, u32[]{:S(2)}) copy-start(f32[1,1,512]{2,1,0:T(1,128)S(1)} %get-tuple-element.73) | copy-start | bytes 6148
  22.1 75.0 %copy-start.81 = (f32[1,1,512]{2,1,0:T(1,128)}, f32[1,1,512]{2,1,0:T(1,128)S(1)}, u32[]{:S(2)}) copy-start(f32[1,1,512]{2,1,0:T(1,128)S(1)} %get-tuple-element.72) | copy-start | bytes 6148
  22.1 39.1 %copy-start.94 = (f32[1,1,512]{2,1,0:T(1,128)}, f32[1,1,512]{2,1,0:T(1,128)S(1)}, u32[]{:S(2)}) copy-start(f32[1,1,512]{2,1,0:T(1,128)S(1)} %get-tuple-element.75) | copy-start | bytes 6148
  22.4 38.8 %copy-start.77 = (f32[788]{0:T(1024)}, f32[788]{0:T(1024)S(1)}, u32[]{:S(2)}) copy-start(f32[788]{0:T(1024)S(1)} %broadcast_multiply_fusion.3) | copy-start | bytes 9460
  22.8 38.4 %copy-start.83 = (f32[788]{0:T(1024)}, f32[788]{0:T(1024)S(1)}, u32[]{:S(2)}) copy-start(f32[788]{0:T(1024)S(1)} %fusion.115) | copy-start | bytes 9460
  23.7 19.3 %copy-start.101 = (s32[2]{0:T(128)S(1)}, s32[2]{0:T(128)}, u32[]{:S(2)}) copy-start(s32[2]{0:T(128)} %constant.144) | copy-start | bytes 28
  23.7 19.4 %copy-start.100 = (s32[2]{0:T(128)S(1)}, s32[2]{0:T(128)}, u32[]{:S(2)}) copy-start(s32[2]{0:T(128)} %constant.141) | copy-start | bytes 28
  98.2 118.8 %copy-start.24 = (bf16[788,512]{1,0:T(8,128)(2,1)}, bf16[788,512]{1,0:T(8,128)(2,1)S(1)}, u32[]{:S(2)}) copy-start(bf16[788,512]{1,0:T(8,128)(2,1)S(1)} %add_convert_fusion.2) | copy-start | bytes 2420740
  107.8 54.9 %all-to-all-start = ((bf16[8,2,128,512]{3,2,1,0:T(8,128)(2,1)}), bf16[8,2,128,512]{3,2,1,0:T(8,128)(2,1)}, u32[]{:S(2)}, u32[]{:S(2)}) async-start(bf16[8,2,128,512]{3,2,1,0:T(8,128)(2,1)} %bitcast.298), calls=%async_computation | async-start | bytes 4194304 | tf_op jit(solution)/shard_map/all_to_all | solution.py:125
  113.9 63.0 %all-gather.25.cloned.1.call-start = ((), (), s32[]{:S(2)}) async-start(), calls=%async_computation.32 | async-start | bytes 2621440 | tf_op jit(solution)/shard_map/all_gather | solution.py:314
  186.8 52.4 %all-to-all-start.1 = ((bf16[8,2,128,512]{3,2,1,0:T(8,128)(2,1)}), bf16[8,2,128,512]{3,2,1,0:T(8,128)(2,1)}, u32[]{:S(2)}, u32[]{:S(2)}) async-start(bf16[8,2,128,512]{3,2,1,0:T(8,128)(2,1)} %bitcast.306), calls=%async_computation.1 | async-start | bytes 4194304 | tf_op jit(solution)/shard_map/all_to_all | solution.py:132
  191.2 66.0 %all-gather.27.cloned.1.call-start = ((), (), s32[]{:S(2)}) async-start(), calls=%async_computation.33 | async-start | bytes 1966080 | tf_op jit(solution)/shard_map/all_gather | solution.py:310
  207.9 32.9 %copy-start.65 = (bf16[1,512,8]{1,2,0:T(8,128)(2,1)}, bf16[1,512,8]{1,2,0:T(8,128)(2,1)S(1)}, u32[]{:S(2)}) copy-start(bf16[1,512,8]{1,2,0:T(8,128)(2,1)S(1)} %all-gather.4) | copy-start | bytes 24580
  216.9 40.3 %copy-start.89 = (f32[1,1,512]{2,1,0:T(1,128)}, f32[1,1,512]{2,1,0:T(1,128)S(1)}, u32[]{:S(2)}) copy-start(f32[1,1,512]{2,1,0:T(1,128)S(1)} %get-tuple-element.69) | copy-start | bytes 6148
  217.0 40.3 %copy-start.96 = (f32[1,1,512]{2,1,0:T(1,128)}, f32[1,1,512]{2,1,0:T(1,128)S(1)}, u32[]{:S(2)}) copy-start(f32[1,1,512]{2,1,0:T(1,128)S(1)} %get-tuple-element.71) | copy-start | bytes 6148
  217.3 23.6 %copy-start.61 = (f32[788]{0:T(1024)}, f32[788]{0:T(1024)S(1)}, u32[]{:S(2)}) copy-start(f32[788]{0:T(1024)S(1)} %get-tuple-element.86) | copy-start | bytes 9460
  256.8 34.4 %copy-start.11 = (f32[788,512]{1,0:T(8,128)}, f32[788,512]{1,0:T(8,128)S(1)}, u32[]{:S(2)}) copy-start(f32[788,512]{1,0:T(8,128)S(1)} %get-tuple-element.42) | copy-start | bytes 4841476
  293.6 26.8 %copy-start.25 = (bf16[788,512]{1,0:T(8,128)(2,1)}, bf16[788,512]{1,0:T(8,128)(2,1)S(1)}, u32[]{:S(2)}) copy-start(bf16[788,512]{1,0:T(8,128)(2,1)S(1)} %add_convert_fusion) | copy-start | bytes 2420740
  303.3 52.2 %all-to-all-start.2 = ((bf16[8,2,128,512]{3,2,1,0:T(8,128)(2,1)}), bf16[8,2,128,512]{3,2,1,0:T(8,128)(2,1)}, u32[]{:S(2)}, u32[]{:S(2)}) async-start(bf16[8,2,128,512]{3,2,1,0:T(8,128)(2,1)} %bitcast.296), calls=%async_computation.2 | async-start | bytes 4194304 | tf_op jit(solution)/shard_map/all_to_all | solution.py:125
  307.6 52.0 %all-gather.29.cloned.1.call-start = ((), (), s32[]{:S(2)}) async-start(), calls=%async_computation.34 | async-start | bytes 2621440 | tf_op jit(solution)/shard_map/all_gather | solution.py:313
  355.4 52.0 %all-to-all-start.4 = ((bf16[8,2,128,512]{3,2,1,0:T(8,128)(2,1)}), bf16[8,2,128,512]{3,2,1,0:T(8,128)(2,1)S(1)}, u32[]{:S(2)}, u32[]{:S(2)}) async-start(bf16[8,2,128,512]{3,2,1,0:T(8,128)(2,1)} %bitcast.297), calls=%async_computation.4 | async-start | bytes 4194304 | tf_op jit(solution)/shard_map/all_to_all | solution.py:208
  359.1 26.1 %all-gather.31.cloned.1.call-start = ((), (), s32[]{:S(2)}) async-start(), calls=%async_computation.35 | async-start | bytes 2621440 | tf_op jit(solution)/shard_map/all_gather | solution.py:314
  407.5 17.2 %copy-start.49 = (bf16[8,2,128,512]{3,2,1,0:T(8,128)(2,1)}, bf16[8,2,128,512]{3,2,1,0:T(8,128)(2,1)S(1)}, u32[]{:S(2)}) copy-start(bf16[8,2,128,512]{3,2,1,0:T(8,128)(2,1)S(1)} %all-to-all-done.4) | copy-start | bytes 6291460
  407.5 17.2 %copy-start.104 = (bf16[1,1,512,2048]{3,2,1,0:T(8,128)(2,1)S(1)}, bf16[1,1,512,2048]{3,2,1,0:T(8,128)(2,1)}, u32[]{:S(2)}) copy-start(bf16[1,1,512,2048]{3,2,1,0:T(8,128)(2,1)} %all-gather.29.cloned.1.call-done) | copy-start | bytes 6291460
  430.7 52.1 %all-to-all-start.5 = ((bf16[8,2,128,512]{3,2,1,0:T(8,128)(2,1)}), bf16[8,2,128,512]{3,2,1,0:T(8,128)(2,1)S(1)}, u32[]{:S(2)}, u32[]{:S(2)}) async-start(bf16[8,2,128,512]{3,2,1,0:T(8,128)(2,1)} %bitcast.308), calls=%async_computation.5 | async-start | bytes 4194304 | tf_op jit(solution)/shard_map/all_to_all | solution.py:216
  484.1 52.4 %all-to-all-start.3 = ((bf16[8,2,128,512]{3,2,1,0:T(8,128)(2,1)}), bf16[8,2,128,512]{3,2,1,0:T(8,128)(2,1)}, u32[]{:S(2)}, u32[]{:S(2)}) async-start(bf16[8,2,128,512]{3,2,1,0:T(8,128)(2,1)} %bitcast.307), calls=%async_computation.3 | async-start | bytes 4194304 | tf_op jit(solution)/shard_map/all_to_all | solution.py:132
  618.4 52.1 %copy-start.103 = (bf16[1,1,2048,512]{3,2,1,0:T(8,128)(2,1)S(1)}, bf16[1,1,2048,512]{3,2,1,0:T(8,128)(2,1)}, u32[]{:S(2)}) copy-start(bf16[1,1,2048,512]{3,2,1,0:T(8,128)(2,1)} %all-gather.25.cloned.1.call-done) | copy-start | bytes 6291460
  670.5 17.5 %copy-start.50 = (bf16[8,2,128,512]{3,2,1,0:T(8,128)(2,1)}, bf16[8,2,128,512]{3,2,1,0:T(8,128)(2,1)S(1)}, u32[]{:S(2)}) copy-start(bf16[8,2,128,512]{3,2,1,0:T(8,128)(2,1)S(1)} %all_to_all.40) | copy-start | bytes 6291460
  670.5 17.5 %copy-start.102 = (bf16[1,1,512,2048]{3,2,1,0:T(8,128)(2,1)S(1)}, bf16[1,1,512,2048]{3,2,1,0:T(8,128)(2,1)}, u32[]{:S(2)}) copy-start(bf16[1,1,512,2048]{3,2,1,0:T(8,128)(2,1)} %all-gather.23.cloned.1.call-done) | copy-start | bytes 6291460
  694.1 51.9 %all-to-all-start.7 = ((bf16[8,2,128,512]{3,2,1,0:T(8,128)(2,1)}), bf16[8,2,128,512]{3,2,1,0:T(8,128)(2,1)}, u32[]{:S(2)}, u32[]{:S(2)}) async-start(bf16[8,2,128,512]{3,2,1,0:T(8,128)(2,1)} %bitcast.305), calls=%async_computation.7 | async-start | bytes 4194304 | tf_op jit(solution)/shard_map/all_to_all | solution.py:216
  698.7 156.1 %reduce-scatter.49.cloned.1.call-start = ((), (), s32[]{:S(2)}) async-start(), calls=%async_computation.39 | async-start | bytes 163840
  699.7 156.0 %reduce-scatter.45.cloned.1.call-start = ((), (), s32[]{:S(2)}) async-start(), calls=%async_computation.37 | async-start | bytes 163840
  700.6 155.9 %reduce-scatter.53.cloned.1.call-start = ((), (), s32[]{:S(2)}) async-start(), calls=%async_computation.41 | async-start | bytes 163840
  703.8 153.5 %reduce-scatter.51.cloned.1.call-start = ((), (), s32[]{:S(2)}) async-start(), calls=%async_computation.40 | async-start | bytes 163840
  706.4 155.1 %reduce-scatter.33.cloned.1.call-start = ((), (), s32[]{:S(2)}) async-start(), calls=%async_computation.25 | async-start | bytes 655360 | tf_op jit(solution)/shard_map/reduce_scatter | solution.py:272
  709.1 152.3 %reduce-scatter.29.cloned.1.call-start = ((), (), s32[]{:S(2)}) async-start(), calls=%async_computation.23 | async-start | bytes 1966080 | tf_op jit(solution)/shard_map/reduce_scatter | solution.py:272
  714.4 154.6 %reduce-scatter.31.cloned.1.call-start = ((), (), s32[]{:S(2)}) async-start(), calls=%async_computation.24 | async-start | bytes 655360 | tf_op jit(solution)/shard_map/reduce_scatter | solution.py:272
  780.8 118.7 %reduce-scatter.27.cloned.1.call-start = ((), (), s32[]{:S(2)}) async-start(), calls=%async_computation.22 | async-start | bytes 1966080 | tf_op jit(solution)/shard_map/reduce_scatter | solution.py:272
  807.6 113.8 %reduce-scatter.47.cloned.1.call-start = ((), (), s32[]{:S(2)}) async-start(), calls=%async_computation.38 | async-start | bytes 163840
  813.4 129.9 %reduce-scatter.43.cloned.1.call-start = ((), (), s32[]{:S(2)}) async-start(), calls=%async_computation.36 | async-start | bytes 163840
  814.3 163.2 %reduce-scatter.41.cloned.1.call-start = ((), (), s32[]{:S(2)}) async-start(), calls=%async_computation.29 | async-start | bytes 2621440 | tf_op jit(solution)/shard_map/reduce_scatter | solution.py:272
  824.4 186.7 %reduce-scatter.39.cloned.1.call-start = ((), (), s32[]{:S(2)}) async-start(), calls=%async_computation.28 | async-start | bytes 2621440 | tf_op jit(solution)/shard_map/reduce_scatter | solution.py:272
  834.6 210.8 %reduce-scatter.37.cloned.1.call-start = ((), (), s32[]{:S(2)}) async-start(), calls=%async_computation.27 | async-start | bytes 2621440 | tf_op jit(solution)/shard_map/reduce_scatter | solution.py:272
  844.8 234.2 %reduce-scatter.35.cloned.1.call-start = ((), (), s32[]{:S(2)}) async-start(), calls=%async_computation.26 | async-start | bytes 2621440 | tf_op jit(solution)/shard_map/reduce_scatter | solution.py:272
  854.8 306.4 %all-reduce.12.cloned.1.call-start = ((), (), s32[]{:S(2)}) async-start(), calls=%async_computation.42 | async-start | bytes 2097152 | tf_op jit(solution)/shard_map/psum | solution.py:278
  858.2 41.3 %copy-start.15 = (f32[788,512]{1,0:T(8,128)S(1)}, f32[788,512]{1,0:T(8,128)}, u32[]{:S(2)}) copy-start(f32[788,512]{1,0:T(8,128)} %copy-done.14) | copy-start | bytes 4841476
  (93 other events, 376.1 us)
Sparse Core Ops, SparseCore 0:
  10.2 22.3 all-gather.20
  34.7 22.5 all-gather.22
  116.8 23.9 all-gather.24
  193.3 22.2 all-gather.26
  310.3 23.8 all-gather.28
  361.1 23.9 all-gather.30
  702.0 20.9 reduce-scatter.48
  725.4 19.6 reduce-scatter.44
  747.5 19.6 reduce-scatter.52
  769.4 19.6 reduce-scatter.50
  792.2 21.6 reduce-scatter.32
  816.8 28.0 reduce-scatter.28
  847.4 21.6 reduce-scatter.30
  871.4 28.0 reduce-scatter.26
  901.8 19.6 reduce-scatter.46
  923.7 19.6 reduce-scatter.42
  946.3 31.1 reduce-scatter.40
  979.9 31.1 reduce-scatter.38
  1014.2 31.1 reduce-scatter.36
  1047.8 31.1 reduce-scatter.34
  1082.8 78.2 all-reduce.11
where the time goes:
time: 1180 us; the launch traced here: 1170 us
  waiting for transfers between devices  502 us (43%)
  local copies, waits for them, and re-layouts  218 us (18%)
  matrix products  206 us (17%)
  blocking collectives  123 us (10%)
  other arithmetic  72.7 us (6%)
  starting transfers between devices  33.4 us (3%)
  between operations  16.5 us (1%)
    reduce_scatter x8, waiting for transfers between devices, reduce_layer(): lax.psum_scatter(grad.astype(jnp.bfloat16), 'shard', scatter_dimension=di...  147 us
    psum x1, waiting for transfers between devices, reduce_layer(): lax.psum(part.astype(jnp.bfloat16), 'expert').astype(jnp.float32)  79.5 us
    all_to_all x2, waiting for transfers between devices, backward_layer(): lax.all_to_all(d_rows, 'expert', split_axis=0, concat_axis=0, tiled=True)  70.1 us
    all_to_all x2, waiting for transfers between devices, forward_layer(): lax.all_to_all(sending, 'expert', split_axis=0, concat_axis=0, tiled=True)  70 us
    all_to_all x2, waiting for transfers between devices, forward_layer(): lax.all_to_all(expert_rows.reshape(experts, blocks, capacity, D), 'expert...  60.4 us
    dot_general x10, matrix products, dot_last(): lax.dot_general(left, right, (((1,), (1,)), ((), ())), preferred_element_...  58.6 us
    dot_general x10, matrix products, dot_first(): lax.dot_general(left, right, (((0,), (0,)), ((), ())), preferred_element_...  57.7 us
    all_to_all x1, blocking collectives, backward_layer(): lax.all_to_all(d_slots, 'expert', split_axis=0, concat_axis=0, tiled=True)  52.1 us
  transfers between devices with their start and end apart: 28, of which 17 were waited for; matrix products, arithmetic and copies ran while one was open for 25% of the time, Pallas kernels for 0%

commit v1 on v0

--- a/solution.py
+++ b/solution.py
@@ -275,7 +275,8 @@
         for grad, dim in zip(layer_grads, SCATTER_DIMS)
     ]
     replicated = [
-        lax.psum(part.astype(jnp.bfloat16), "expert").astype(jnp.float32) for part in scattered[:5]
+        jnp.sum(lax.all_gather(part.astype(jnp.bfloat16), "expert"), axis=0).astype(jnp.float32)
+        for part in scattered[:5]
     ]
     return replicated + scattered[5:]
 

time: 1180 us -> 1330 us (1.13)
  blocking collectives: 123 us -> 232 us
  waiting for transfers between devices: 502 us -> 538 us
    all_gather x0 -> x4, waiting for transfers between devices: none -> 157 us  [reduce_layer(): lax.all_gather(part.astype(jnp.bfloat16), 'expert')]
    all_gather x0 -> x6, blocking collectives: none -> 131 us  [reduce_layer(): lax.all_gather(part.astype(jnp.bfloat16), 'expert')]
    psum x1 -> x0, waiting for transfers between devices: 79.5 us -> none  [reduce_layer(): lax.psum(part.astype(jnp.bfloat16), 'expert').astype(jnp.float32)]
    reduce_scatter x8, waiting for transfers between devices: 147 us -> 111 us  [reduce_layer(): lax.psum_scatter(grad.astype(jnp.bfloat16), 'shard', scatter_dimension=di...]
    psum x1 -> x0, blocking collectives: 21.6 us -> none  [reduce_layer(): lax.psum(part.astype(jnp.bfloat16), 'expert').astype(jnp.float32)]
    unnamed x27 -> x30, waiting for transfers between devices: 42.1 us -> 32 us
    unnamed x251 -> x255, local copies, waits for them, and re-layouts: 49 us -> 48.8 us
  transfers between devices with their start and end apart: 28 -> 31, of which waited for: 17 -> 19; matrix products, arithmetic and copies ran while one was open for 25% -> 23% of each run, Pallas kernels for 0% -> 0%
where the time goes in v1:
time: 1330 us; the launch traced here: 1320 us
  waiting for transfers between devices  538 us (40%)
  blocking collectives  232 us (17%)
  local copies, waits for them, and re-layouts  218 us (16%)
  matrix products  206 us (15%)
  other arithmetic  74.3 us (6%)
  starting transfers between devices  33.4 us (3%)
  between operations  16.6 us (1%)
    all_gather x4, waiting for transfers between devices, reduce_layer(): lax.all_gather(part.astype(jnp.bfloat16), 'expert')  157 us
    all_gather x6, blocking collectives, reduce_layer(): lax.all_gather(part.astype(jnp.bfloat16), 'expert')  131 us
    reduce_scatter x8, waiting for transfers between devices, reduce_layer(): lax.psum_scatter(grad.astype(jnp.bfloat16), 'shard', scatter_dimension=di...  111 us
    all_to_all x2, waiting for transfers between devices, backward_layer(): lax.all_to_all(d_rows, 'expert', split_axis=0, concat_axis=0, tiled=True)  74.3 us
    all_to_all x2, waiting for transfers between devices, forward_layer(): lax.all_to_all(sending, 'expert', split_axis=0, concat_axis=0, tiled=True)  70 us
    all_to_all x2, waiting for transfers between devices, forward_layer(): lax.all_to_all(expert_rows.reshape(experts, blocks, capacity, D), 'expert...  61 us
    dot_general x10, matrix products, dot_last(): lax.dot_general(left, right, (((1,), (1,)), ((), ())), preferred_element_...  58.8 us
    dot_general x10, matrix products, dot_first(): lax.dot_general(left, right, (((0,), (0,)), ((), ())), preferred_element_...  57.5 us
  transfers between devices with their start and end apart: 31, of which 19 were waited for; matrix products, arithmetic and copies ran while one was open for 23% of the time, Pallas kernels for 0%

profile of v1, /device:TPU:0, one launch (start us, length us, event | category | flops | bytes accessed | tf_op | source)
XLA Modules:
  0.0 1318.8 jit_solution(10368019118343551874)
XLA Ops:
  24.2 16.5 %fusion.16 = s32[2,788]{0,1:T(8,128)S(1)} fusion(s32[2,788]{0,1:T(8,128)S(1)} %copy.267, s32[2,788]{1,0:T(2,128)S(1)} %get-tuple-element.95, s32[2,788]{1,0:T(2,128)S(1)} %get-tuple-element.94, s32[2,788]{0,1:T(8,128)S(1)} %copy.266), kind=kLoop, calls=%fused_computation.42 | loop fusion | flops 6207864 | bytes 31520 | tf_op jit(solution)/shard_map/vmap()/reduce_sum | solution.py:47
  43.9 8.8 scatter_custom_fusion
  52.9 8.3 all-gather.3
  65.6 7.2 reshape.825
  98.7 9.2 gather_fusion
  107.9 6.1 all-to-all-start
  115.3 47.5 %all-to-all-done = bf16[8,2,128,512]{3,2,1,0:T(8,128)(2,1)} async-done(((bf16[8,2,128,512]{3,2,1,0:T(8,128)(2,1)}), bf16[8,2,128,512]{3,2,1,0:T(8,128)(2,1)}, u32[]{:S(2)}, u32[]{:S(2)}) %all-to-all-start) | async-done | bytes 2097184 | tf_op jit(solution)/shard_map/all_to_all | solution.py:125
  162.8 14.1 %multiply_convert_fusion.1 = (bf16[2048,2048]{1,0:T(8,128)(2,1)}, f32[2048,2048]{1,0:T(8,128)}) fusion(bf16[2048,512]{1,0:T(8,128)(2,1)} %bitcast.20, bf16[1,1,512,2048]{3,2,1,0:T(8,128)(2,1)} %all-gather.41.cloned.1.call-done), kind=kOutput, calls=%fused_computation.28 | convolution fusion | flops 4332716032 | bytes 29360128 | tf_op jit(solution)/shard_map/dot_general | solution.py:127
  176.9 9.8 convolution_convert_fusion.11
  207.9 9.0 all-gather.10
  218.0 21.0 %all-to-all-done.1 = bf16[8,2,128,512]{3,2,1,0:T(8,128)(2,1)} async-done(((bf16[8,2,128,512]{3,2,1,0:T(8,128)(2,1)}), bf16[8,2,128,512]{3,2,1,0:T(8,128)(2,1)}, u32[]{:S(2)}, u32[]{:S(2)}) %all-to-all-start.1) | async-done | bytes 2097184 | tf_op jit(solution)/shard_map/all_to_all | solution.py:132
  240.8 6.4 gather_fusion.1
  261.6 7.2 reshape.826
  294.0 9.2 gather_fusion.2
  323.7 9.2 gather_fusion.4
  332.9 22.5 %all-to-all-done.2 = bf16[8,2,128,512]{3,2,1,0:T(8,128)(2,1)} async-done(((bf16[8,2,128,512]{3,2,1,0:T(8,128)(2,1)}), bf16[8,2,128,512]{3,2,1,0:T(8,128)(2,1)}, u32[]{:S(2)}, u32[]{:S(2)}) %all-to-all-start.2) | async-done | bytes 2097184 | tf_op jit(solution)/shard_map/all_to_all | solution.py:125
  359.6 14.4 %multiply_convert_fusion = (bf16[2048,2048]{1,0:T(8,128)(2,1)}, f32[2048,2048]{1,0:T(8,128)}) fusion(bf16[2048,512]{1,0:T(8,128)(2,1)} %bitcast.38, bf16[1,1,512,2048]{3,2,1,0:T(8,128)(2,1)} %all-gather.47.cloned.1.call-done), kind=kOutput, calls=%fused_computation.27 | convolution fusion | flops 4332716032 | bytes 29360128 | tf_op jit(solution)/shard_map/dot_general | solution.py:127
  374.0 11.0 all-gather.49.cloned.1.call-done
  385.1 22.3 %all-to-all-done.4 = bf16[8,2,128,512]{3,2,1,0:T(8,128)(2,1)S(1)} async-done(((bf16[8,2,128,512]{3,2,1,0:T(8,128)(2,1)}), bf16[8,2,128,512]{3,2,1,0:T(8,128)(2,1)S(1)}, u32[]{:S(2)}, u32[]{:S(2)}) %all-to-all-start.4) | async-done | bytes 2097184 | tf_op jit(solution)/shard_map/all_to_all | solution.py:208
  407.4 17.1 %fusion.13 = bf16[2048,2048]{1,0:T(8,128)(2,1)S(1)} fusion(f32[2048,2048]{1,0:T(8,128)} %get-tuple-element.85, bf16[2048,512]{1,0:T(8,128)(2,1)S(1)} %bitcast.315, bf16[1,1,2048,512]{3,2,1,0:T(8,128)(2,1)} %all-gather.49.cloned.1.call-done), kind=kOutput, calls=%fused_computation.26 | convolution fusion | flops 4378853376 | bytes 29360128 | tf_op jit(solution)/shard_map/dot_general | solution.py:36
  434.3 9.8 convolution_convert_fusion.10
  444.1 38.6 %all-to-all-done.5 = bf16[8,2,128,512]{3,2,1,0:T(8,128)(2,1)S(1)} async-done(((bf16[8,2,128,512]{3,2,1,0:T(8,128)(2,1)}), bf16[8,2,128,512]{3,2,1,0:T(8,128)(2,1)S(1)}, u32[]{:S(2)}, u32[]{:S(2)}) %all-to-all-start.5) | async-done | bytes 2097184 | tf_op jit(solution)/shard_map/all_to_all | solution.py:216
  496.5 39.9 %all-to-all-done.3 = bf16[8,2,128,512]{3,2,1,0:T(8,128)(2,1)} async-done(((bf16[8,2,128,512]{3,2,1,0:T(8,128)(2,1)}), bf16[8,2,128,512]{3,2,1,0:T(8,128)(2,1)}, u32[]{:S(2)}, u32[]{:S(2)}) %all-to-all-start.3) | async-done | bytes 2097184 | tf_op jit(solution)/shard_map/all_to_all | solution.py:132
  587.9 7.0 convert_element_type.400
  609.3 9.2 gather_fusion.6
  618.5 52.1 %all_to_all.40 = bf16[8,2,128,512]{3,2,1,0:T(8,128)(2,1)S(1)} all-to-all(bf16[8,2,128,512]{3,2,1,0:T(8,128)(2,1)} %bitcast.311), channel_id=1, replica_groups=mesh['expert'=8,'shard'=4] {'expert'}, dimensions={0} | all-to-all | bytes 4194304 | tf_op jit(solution)/shard_map/all_to_all | solution.py:208
  670.6 17.5 %fusion.6 = bf16[2048,2048]{1,0:T(8,128)(2,1)S(1)} fusion(f32[2048,2048]{1,0:T(8,128)} %get-tuple-element.75, bf16[2048,512]{1,0:T(8,128)(2,1)S(1)} %bitcast.317, bf16[1,1,2048,512]{3,2,1,0:T(8,128)(2,1)S(1)} %copy-done.106), kind=kOutput, calls=%fused_computation.19 | convolution fusion | flops 4378853376 | bytes 29360128 | tf_op jit(solution)/shard_map/dot_general | solution.py:36
  710.3 35.7 %all-to-all-done.7 = bf16[8,2,128,512]{3,2,1,0:T(8,128)(2,1)} async-done(((bf16[8,2,128,512]{3,2,1,0:T(8,128)(2,1)}), bf16[8,2,128,512]{3,2,1,0:T(8,128)(2,1)}, u32[]{:S(2)}, u32[]{:S(2)}) %all-to-all-start.7) | async-done | bytes 2097184 | tf_op jit(solution)/shard_map/all_to_all | solution.py:216
  781.1 6.4 multiply_convert_fusion.2
  795.2 6.9 convert_element_type.411
  818.8 9.9 fusion.32
  828.7 9.9 fusion.31
  839.0 9.9 fusion.30
  849.0 10.0 fusion.29
  861.9 18.6 %all-gather.27 = bf16[8,2,128]{2,1,0:T(2,128)(2,1)S(1)} all-gather(bf16[1,2,128]{2,1,0:T(2,128)(2,1)S(1)} %bitcast.360), channel_id=19, replica_groups=mesh['expert'=8,'shard'=4] {'expert'}, dimensions={0}, use_global_device_ids=true | all-gather | bytes 4608 | tf_op jit(solution)/shard_map/all_gather | solution.py:278
  881.3 18.7 %all-gather.25 = bf16[8,2,128]{2,1,0:T(2,128)(2,1)S(1)} all-gather(bf16[1,2,128]{2,1,0:T(2,128)(2,1)S(1)} %bitcast.361), channel_id=17, replica_groups=mesh['expert'=8,'shard'=4] {'expert'}, dimensions={0}, use_global_device_ids=true | all-gather | bytes 4608 | tf_op jit(solution)/shard_map/all_gather | solution.py:278
  901.6 21.1 %reduce-scatter.51.cloned.1.call-done = bf16[128,8]{1,0:T(8,128)(2,1)} async-done(((bf16[512,8]{1,0:T(8,128)(2,1)}), bf16[128,8]{1,0:T(8,128)(2,1)}) %reduce-scatter.51.cloned.1.call-update) | async-done | bytes 2064
  923.6 26.2 %all-gather.23 = bf16[1024,8]{0,1:T(8,128)(2,1)S(1)} all-gather(bf16[128,8]{0,1:T(8,128)(2,1)S(1)} %copy.320), channel_id=25, replica_groups=mesh['expert'=8,'shard'=4] {'expert'}, dimensions={0}, use_global_device_ids=true | all-gather | bytes 18432 | tf_op jit(solution)/shard_map/all_gather | solution.py:278
  949.8 26.3 %all-gather.22 = bf16[1024,8]{0,1:T(8,128)(2,1)S(1)} all-gather(bf16[128,8]{0,1:T(8,128)(2,1)S(1)} %copy.318), channel_id=24, replica_groups=mesh['expert'=8,'shard'=4] {'expert'}, dimensions={0}, use_global_device_ids=true | all-gather | bytes 18432 | tf_op jit(solution)/shard_map/all_gather | solution.py:278
  986.5 20.5 %all-gather.26 = bf16[8,2,128]{2,1,0:T(2,128)(2,1)S(1)} all-gather(bf16[1,2,128]{2,1,0:T(2,128)(2,1)S(1)} %bitcast.362), channel_id=18, replica_groups=mesh['expert'=8,'shard'=4] {'expert'}, dimensions={0}, use_global_device_ids=true | all-gather | bytes 4608 | tf_op jit(solution)/shard_map/all_gather | solution.py:278
  1009.0 20.5 %all-gather.24 = bf16[8,2,128]{2,1,0:T(2,128)(2,1)S(1)} all-gather(bf16[1,2,128]{2,1,0:T(2,128)(2,1)S(1)} %bitcast.363), channel_id=16, replica_groups=mesh['expert'=8,'shard'=4] {'expert'}, dimensions={0}, use_global_device_ids=true | all-gather | bytes 4608 | tf_op jit(solution)/shard_map/all_gather | solution.py:278
  1030.7 11.6 reduce-scatter.41.cloned.1.call-done
  1042.4 33.7 %reduce-scatter.39.cloned.1.call-done = bf16[1,512,512]{2,1,0:T(8,128)(2,1)} async-done(((bf16[1,2048,512]{2,1,0:T(8,128)(2,1)}), bf16[1,512,512]{2,1,0:T(8,128)(2,1)}) %reduce-scatter.39.cloned.1.call-update) | async-done | bytes 524304 | tf_op jit(solution)/shard_map/reduce_scatter | solution.py:272
  1078.7 31.5 %reduce-scatter.37.cloned.1.call-done = bf16[1,128,2048]{2,1,0:T(8,128)(2,1)} async-done(((bf16[1,512,2048]{2,1,0:T(8,128)(2,1)}), bf16[1,128,2048]{2,1,0:T(8,128)(2,1)}) %reduce-scatter.37.cloned.1.call-update) | async-done | bytes 524304 | tf_op jit(solution)/shard_map/reduce_scatter | solution.py:272
  1110.2 33.7 %reduce-scatter.35.cloned.1.call-done = bf16[1,128,2048]{2,1,0:T(8,128)(2,1)} async-done(((bf16[1,512,2048]{2,1,0:T(8,128)(2,1)}), bf16[1,128,2048]{2,1,0:T(8,128)(2,1)}) %reduce-scatter.35.cloned.1.call-update) | async-done | bytes 524304 | tf_op jit(solution)/shard_map/reduce_scatter | solution.py:272
  1146.6 59.6 %all-gather.53.cloned.1.call-done = bf16[1024,1536]{1,0:T(8,128)(2,1)} async-done(((bf16[128,1536]{1,0:T(8,128)(2,1)}), bf16[1024,1536]{1,0:T(8,128)(2,1)}) %all-gather.53.cloned.1.call-update) | async-done | bytes 3145744 | tf_op jit(solution)/shard_map/all_gather | solution.py:278
  1208.6 38.7 %all-gather.55.cloned.1.call-done = bf16[1024,512]{1,0:T(8,128)(2,1)} async-done(((bf16[128,512]{1,0:T(8,128)(2,1)}), bf16[1024,512]{1,0:T(8,128)(2,1)}) %all-gather.55.cloned.1.call-update) | async-done | bytes 1048592 | tf_op jit(solution)/shard_map/all_gather | solution.py:278
  1249.5 58.6 %all-gather.51.cloned.1.call-done = bf16[1024,1536]{1,0:T(8,128)(2,1)} async-done(((bf16[128,1536]{1,0:T(8,128)(2,1)}), bf16[1024,1536]{1,0:T(8,128)(2,1)}) %all-gather.51.cloned.1.call-update) | async-done | bytes 3145744 | tf_op jit(solution)/shard_map/all_gather | solution.py:278
  (545 shorter events, 342.9 us)
Async XLA Ops:
  7.2 54.0 %all-gather.39.cloned.1.call-start = ((), (), s32[]{:S(2)}) async-start(), calls=%async_computation.30 | async-start | bytes 1966080 | tf_op jit(solution)/shard_map/all_gather | solution.py:311
  9.5 105.8 %all-gather.41.cloned.1.call-start = ((), (), s32[]{:S(2)}) async-start(), calls=%async_computation.31 | async-start | bytes 2621440 | tf_op jit(solution)/shard_map/all_gather | solution.py:314
  22.1 39.1 %copy-start.88 = (f32[1,1,512]{2,1,0:T(1,128)}, f32[1,1,512]{2,1,0:T(1,128)S(1)}, u32[]{:S(2)}) copy-start(f32[1,1,512]{2,1,0:T(1,128)S(1)} %get-tuple-element.63) | copy-start | bytes 6148
  22.1 75.8 %copy-start.82 = (f32[1,1,512]{2,1,0:T(1,128)}, f32[1,1,512]{2,1,0:T(1,128)S(1)}, u32[]{:S(2)}) copy-start(f32[1,1,512]{2,1,0:T(1,128)S(1)} %get-tuple-element.62) | copy-start | bytes 6148
  22.1 39.1 %copy-start.97 = (f32[1,1,512]{2,1,0:T(1,128)}, f32[1,1,512]{2,1,0:T(1,128)S(1)}, u32[]{:S(2)}) copy-start(f32[1,1,512]{2,1,0:T(1,128)S(1)} %get-tuple-element.65) | copy-start | bytes 6148
  22.4 38.8 %copy-start.78 = (f32[788]{0:T(1024)}, f32[788]{0:T(1024)S(1)}, u32[]{:S(2)}) copy-start(f32[788]{0:T(1024)S(1)} %broadcast_multiply_fusion.3) | copy-start | bytes 9460
  22.8 38.4 %copy-start.84 = (f32[788]{0:T(1024)}, f32[788]{0:T(1024)S(1)}, u32[]{:S(2)}) copy-start(f32[788]{0:T(1024)S(1)} %fusion.115) | copy-start | bytes 9460
  23.7 19.3 %copy-start.104 = (s32[2]{0:T(128)S(1)}, s32[2]{0:T(128)}, u32[]{:S(2)}) copy-start(s32[2]{0:T(128)} %constant.154) | copy-start | bytes 28
  23.7 19.4 %copy-start.103 = (s32[2]{0:T(128)S(1)}, s32[2]{0:T(128)}, u32[]{:S(2)}) copy-start(s32[2]{0:T(128)} %constant.151) | copy-start | bytes 28
  98.2 118.6 %copy-start.22 = (bf16[788,512]{1,0:T(8,128)(2,1)}, bf16[788,512]{1,0:T(8,128)(2,1)S(1)}, u32[]{:S(2)}) copy-start(bf16[788,512]{1,0:T(8,128)(2,1)S(1)} %add_convert_fusion.2) | copy-start | bytes 2420740
  107.9 54.9 %all-to-all-start = ((bf16[8,2,128,512]{3,2,1,0:T(8,128)(2,1)}), bf16[8,2,128,512]{3,2,1,0:T(8,128)(2,1)}, u32[]{:S(2)}, u32[]{:S(2)}) async-start(bf16[8,2,128,512]{3,2,1,0:T(8,128)(2,1)} %bitcast.310), calls=%async_computation | async-start | bytes 4194304 | tf_op jit(solution)/shard_map/all_to_all | solution.py:125
  113.9 62.9 %all-gather.43.cloned.1.call-start = ((), (), s32[]{:S(2)}) async-start(), calls=%async_computation.32 | async-start | bytes 2621440 | tf_op jit(solution)/shard_map/all_gather | solution.py:315
  186.7 52.4 %all-to-all-start.1 = ((bf16[8,2,128,512]{3,2,1,0:T(8,128)(2,1)}), bf16[8,2,128,512]{3,2,1,0:T(8,128)(2,1)}, u32[]{:S(2)}, u32[]{:S(2)}) async-start(bf16[8,2,128,512]{3,2,1,0:T(8,128)(2,1)} %bitcast.319), calls=%async_computation.1 | async-start | bytes 4194304 | tf_op jit(solution)/shard_map/all_to_all | solution.py:132
  191.2 66.0 %all-gather.45.cloned.1.call-start = ((), (), s32[]{:S(2)}) async-start(), calls=%async_computation.33 | async-start | bytes 1966080 | tf_op jit(solution)/shard_map/all_gather | solution.py:311
  207.9 32.9 %copy-start.66 = (bf16[1,512,8]{1,2,0:T(8,128)(2,1)}, bf16[1,512,8]{1,2,0:T(8,128)(2,1)S(1)}, u32[]{:S(2)}) copy-start(bf16[1,512,8]{1,2,0:T(8,128)(2,1)S(1)} %all-gather.4) | copy-start | bytes 24580
  216.9 40.3 %copy-start.90 = (f32[1,1,512]{2,1,0:T(1,128)}, f32[1,1,512]{2,1,0:T(1,128)S(1)}, u32[]{:S(2)}) copy-start(f32[1,1,512]{2,1,0:T(1,128)S(1)} %get-tuple-element.59) | copy-start | bytes 6148
  216.9 40.3 %copy-start.99 = (f32[1,1,512]{2,1,0:T(1,128)}, f32[1,1,512]{2,1,0:T(1,128)S(1)}, u32[]{:S(2)}) copy-start(f32[1,1,512]{2,1,0:T(1,128)S(1)} %get-tuple-element.61) | copy-start | bytes 6148
  217.2 23.6 %copy-start.62 = (f32[788]{0:T(1024)}, f32[788]{0:T(1024)S(1)}, u32[]{:S(2)}) copy-start(f32[788]{0:T(1024)S(1)} %get-tuple-element.76) | copy-start | bytes 9460
  217.9 23.0 %copy-start.68 = (f32[788]{0:T(1024)}, f32[788]{0:T(1024)S(1)}, u32[]{:S(2)}) copy-start(f32[788]{0:T(1024)S(1)} %fusion.104) | copy-start | bytes 9460
  256.7 34.4 %copy-start.11 = (f32[788,512]{1,0:T(8,128)}, f32[788,512]{1,0:T(8,128)S(1)}, u32[]{:S(2)}) copy-start(f32[788,512]{1,0:T(8,128)S(1)} %get-tuple-element.32) | copy-start | bytes 4841476
  293.6 26.8 %copy-start.24 = (bf16[788,512]{1,0:T(8,128)(2,1)}, bf16[788,512]{1,0:T(8,128)(2,1)S(1)}, u32[]{:S(2)}) copy-start(bf16[788,512]{1,0:T(8,128)(2,1)S(1)} %add_convert_fusion) | copy-start | bytes 2420740
  303.2 52.2 %all-to-all-start.2 = ((bf16[8,2,128,512]{3,2,1,0:T(8,128)(2,1)}), bf16[8,2,128,512]{3,2,1,0:T(8,128)(2,1)}, u32[]{:S(2)}, u32[]{:S(2)}) async-start(bf16[8,2,128,512]{3,2,1,0:T(8,128)(2,1)} %bitcast.308), calls=%async_computation.2 | async-start | bytes 4194304 | tf_op jit(solution)/shard_map/all_to_all | solution.py:125
  307.6 52.0 %all-gather.47.cloned.1.call-start = ((), (), s32[]{:S(2)}) async-start(), calls=%async_computation.34 | async-start | bytes 2621440 | tf_op jit(solution)/shard_map/all_gather | solution.py:314
  355.4 52.0 %all-to-all-start.4 = ((bf16[8,2,128,512]{3,2,1,0:T(8,128)(2,1)}), bf16[8,2,128,512]{3,2,1,0:T(8,128)(2,1)S(1)}, u32[]{:S(2)}, u32[]{:S(2)}) async-start(bf16[8,2,128,512]{3,2,1,0:T(8,128)(2,1)} %bitcast.309), calls=%async_computation.4 | async-start | bytes 4194304 | tf_op jit(solution)/shard_map/all_to_all | solution.py:208
  359.0 26.1 %all-gather.49.cloned.1.call-start = ((), (), s32[]{:S(2)}) async-start(), calls=%async_computation.35 | async-start | bytes 2621440 | tf_op jit(solution)/shard_map/all_gather | solution.py:315
  430.7 52.1 %all-to-all-start.5 = ((bf16[8,2,128,512]{3,2,1,0:T(8,128)(2,1)}), bf16[8,2,128,512]{3,2,1,0:T(8,128)(2,1)S(1)}, u32[]{:S(2)}, u32[]{:S(2)}) async-start(bf16[8,2,128,512]{3,2,1,0:T(8,128)(2,1)} %bitcast.321), calls=%async_computation.5 | async-start | bytes 4194304 | tf_op jit(solution)/shard_map/all_to_all | solution.py:216
  484.0 52.4 %all-to-all-start.3 = ((bf16[8,2,128,512]{3,2,1,0:T(8,128)(2,1)}), bf16[8,2,128,512]{3,2,1,0:T(8,128)(2,1)}, u32[]{:S(2)}, u32[]{:S(2)}) async-start(bf16[8,2,128,512]{3,2,1,0:T(8,128)(2,1)} %bitcast.320), calls=%async_computation.3 | async-start | bytes 4194304 | tf_op jit(solution)/shard_map/all_to_all | solution.py:132
  618.5 52.1 %copy-start.106 = (bf16[1,1,2048,512]{3,2,1,0:T(8,128)(2,1)S(1)}, bf16[1,1,2048,512]{3,2,1,0:T(8,128)(2,1)}, u32[]{:S(2)}) copy-start(bf16[1,1,2048,512]{3,2,1,0:T(8,128)(2,1)} %all-gather.43.cloned.1.call-done) | copy-start | bytes 6291460
  694.2 51.8 %all-to-all-start.7 = ((bf16[8,2,128,512]{3,2,1,0:T(8,128)(2,1)}), bf16[8,2,128,512]{3,2,1,0:T(8,128)(2,1)}, u32[]{:S(2)}, u32[]{:S(2)}) async-start(bf16[8,2,128,512]{3,2,1,0:T(8,128)(2,1)} %bitcast.61), calls=%async_computation.7 | async-start | bytes 4194304 | tf_op jit(solution)/shard_map/all_to_all | solution.py:216
  698.7 112.9 %reduce-scatter.33.cloned.1.call-start = ((), (), s32[]{:S(2)}) async-start(), calls=%async_computation.25 | async-start | bytes 655360 | tf_op jit(solution)/shard_map/reduce_scatter | solution.py:272
  702.2 156.9 %reduce-scatter.29.cloned.1.call-start = ((), (), s32[]{:S(2)}) async-start(), calls=%async_computation.23 | async-start | bytes 1966080 | tf_op jit(solution)/shard_map/reduce_scatter | solution.py:272
  710.1 149.7 %reduce-scatter.31.cloned.1.call-start = ((), (), s32[]{:S(2)}) async-start(), calls=%async_computation.24 | async-start | bytes 655360 | tf_op jit(solution)/shard_map/reduce_scatter | solution.py:272
  780.7 79.9 %reduce-scatter.27.cloned.1.call-start = ((), (), s32[]{:S(2)}) async-start(), calls=%async_computation.22 | async-start | bytes 1966080 | tf_op jit(solution)/shard_map/reduce_scatter | solution.py:272
  807.4 53.7 %reduce-scatter.49.cloned.1.call-start = ((), (), s32[]{:S(2)}) async-start(), calls=%async_computation.43 | async-start | bytes 163840
  808.3 72.2 %reduce-scatter.45.cloned.1.call-start = ((), (), s32[]{:S(2)}) async-start(), calls=%async_computation.41 | async-start | bytes 163840
  809.2 91.6 %reduce-scatter.53.cloned.1.call-start = ((), (), s32[]{:S(2)}) async-start(), calls=%async_computation.45 | async-start | bytes 163840
  810.4 112.4 %reduce-scatter.51.cloned.1.call-start = ((), (), s32[]{:S(2)}) async-start(), calls=%async_computation.44 | async-start | bytes 163840
  811.5 165.3 %all-gather.57.cloned.1.call-start = ((), (), s32[]{:S(2)}) async-start(), calls=%async_computation.39 | async-start | bytes 1179648 | tf_op jit(solution)/shard_map/all_gather | solution.py:278
  812.1 173.6 %reduce-scatter.47.cloned.1.call-start = ((), (), s32[]{:S(2)}) async-start(), calls=%async_computation.42 | async-start | bytes 163840
  817.8 190.4 %reduce-scatter.43.cloned.1.call-start = ((), (), s32[]{:S(2)}) async-start(), calls=%async_computation.40 | async-start | bytes 163840
  818.7 223.6 %reduce-scatter.41.cloned.1.call-start = ((), (), s32[]{:S(2)}) async-start(), calls=%async_computation.29 | async-start | bytes 2621440 | tf_op jit(solution)/shard_map/reduce_scatter | solution.py:272
  828.7 247.4 %reduce-scatter.39.cloned.1.call-start = ((), (), s32[]{:S(2)}) async-start(), calls=%async_computation.28 | async-start | bytes 2621440 | tf_op jit(solution)/shard_map/reduce_scatter | solution.py:272
  838.7 271.5 %reduce-scatter.37.cloned.1.call-start = ((), (), s32[]{:S(2)}) async-start(), calls=%async_computation.27 | async-start | bytes 2621440 | tf_op jit(solution)/shard_map/reduce_scatter | solution.py:272
  848.9 295.0 %reduce-scatter.35.cloned.1.call-start = ((), (), s32[]{:S(2)}) async-start(), calls=%async_computation.26 | async-start | bytes 2621440 | tf_op jit(solution)/shard_map/reduce_scatter | solution.py:272
  859.0 119.2 %copy-start.73 = (f32[788]{0:T(1024)S(1)}, f32[788]{0:T(1024)}, u32[]{:S(2)}) copy-start(f32[788]{0:T(1024)} %copy-done.72) | copy-start | bytes 9460
  859.0 347.2 %all-gather.53.cloned.1.call-start = ((), (), s32[]{:S(2)}) async-start(), calls=%async_computation.37 | async-start | bytes 3538944 | tf_op jit(solution)/shard_map/all_gather | solution.py:278
  859.7 387.5 %all-gather.55.cloned.1.call-start = ((), (), s32[]{:S(2)}) async-start(), calls=%async_computation.38 | async-start | bytes 1179648 | tf_op jit(solution)/shard_map/all_gather | solution.py:278
  860.5 447.6 %all-gather.51.cloned.1.call-start = ((), (), s32[]{:S(2)}) async-start(), calls=%async_computation.36 | async-start | bytes 3538944 | tf_op jit(solution)/shard_map/all_gather | solution.py:278
  (98 other events, 455.7 us)
Sparse Core Ops, SparseCore 0:
  10.2 22.3 all-gather.38
  34.7 22.5 all-gather.40
  116.9 23.9 all-gather.42
  193.2 22.2 all-gather.44
  310.2 23.8 all-gather.46
  361.1 23.9 all-gather.48
  702.6 22.9 reduce-scatter.32
  728.7 27.9 reduce-scatter.28
  780.8 20.8 reduce-scatter.30
  807.5 27.1 reduce-scatter.26
  837.1 19.6 reduce-scatter.48
  859.1 19.5 reduce-scatter.44
  881.1 19.6 reduce-scatter.52
  903.1 19.6 reduce-scatter.50
  924.7 40.2 all-gather.56
  967.3 18.3 reduce-scatter.46
  988.5 19.6 reduce-scatter.42
  1011.2 31.1 reduce-scatter.40
  1044.9 31.1 reduce-scatter.38
  1079.0 31.1 reduce-scatter.36
  1112.7 31.1 reduce-scatter.34
  1146.1 60.0 all-gather.52
  1208.3 38.9 all-gather.54
  1249.3 58.7 all-gather.50
